TPU v7x, 256 devices: a whole 4x4x8 slice. The times are simulated.
256 devices in a mesh: seq: 64 (over y, z, core), pb: 4 (over x).
Axes of the slice: x: 4, y: 4, z: 8, core: 2. Of those that a mesh axis runs over, the one named last changes fastest.
Arguments:
- tokens: bfloat16 [16384, 2048], P('seq'), may hold values from -0.119628906 to 0.119628906
- w_query: bfloat16 [2048, 2048], P(None, 'pb')
- w_key: bfloat16 [2048, 2048], P(None, 'pb')
- w_value: bfloat16 [2048, 2048], P(None, 'pb'), may hold values from -0.125 to 0.125
- w_out: bfloat16 [2048, 2048], P('pb'), may hold values from -0.125 to 0.125
- gain_attn: float32 [2048], replicated, may hold values from 0.1 to 1.9
- gain_embed: float32 [2048], replicated, may hold values from 0.1 to 1.9
- queries: bfloat16 [256, 32, 2048], P(('seq', 'pb')), may hold values from -0.125 to 0.125
- query_lengths: int32 [256], P(('seq', 'pb')), may hold values from 8 to 32
- group_lengths: int32 [128], replicated, may hold values from 1 to 1024, 16384 in all
- teacher: float32 [256, 128], P(('seq', 'pb')), may hold values from -12 to 12
Outputs:
- embedded: bfloat16 [16384, 2048], P('seq')
- scores: float32 [256, 128], P(('seq', 'pb'))
- score_gradient: float32 [256, 128], P(('seq', 'pb'))
- distill_loss: float32 [], replicated
Inputs may be any that keep to these rules, and one draw needn't show every extreme that they name: `group_lengths`: the groups cover the document in order: the lengths sum to 16384.
All inputs are finite; a program needn't handle non-finite values.
Results may differ from a plain program's by a relative error of at most 0.013.
Values may be sent and summed in bfloat16 or wider, within the bound.
No kernel may reach another device: no remote copies, remote signals or barrier semaphores. Data moves between devices by JAX's collectives and lax.ppermute only.
A program may use at most 128 MiB of HBM per device.

v0:
```python
import jax
import jax.numpy as jnp
from jax import lax
from jax.sharding import PartitionSpec as P

HD = 128
WIN = 2048
LQ = 32
EPSILON = 1e-06
SOFTMAX_TEMP = 0.1


def shifted_2(x, axis, by):
    count = lax.axis_size(axis)
    pairs = [(i, i + by) for i in range(count) if 0 <= i + by < count]
    return lax.ppermute(x, axis, pairs)


def rms_scale(values, gain):
    mean_sq = jnp.mean(values * values, axis=-1, keepdims=True)
    return values * lax.rsqrt(mean_sq + EPSILON) * gain


def segmented_max(values, group_id):
    span_len = values.shape[-1]
    stride = 1
    while stride < span_len:
        filler = jnp.full(values.shape[:-1] + (stride,), -jnp.inf, values.dtype)
        shifted = jnp.concatenate([filler, values[..., :-stride]], axis=-1)
        prior_id = jnp.concatenate([jnp.full((stride,), -1, jnp.int32), group_id[:-stride]])
        values = jnp.where((prior_id == group_id)[None, :], jnp.maximum(values, shifted), values)
        stride = stride * 2
    return values


def per_device(
    tokens,
    w_query,
    w_key,
    w_value,
    w_out,
    gain_attn,
    gain_embed,
    queries,
    query_lengths,
    group_lengths,
    teacher,
):
    shard_rows = tokens.shape[0]
    seq_count = lax.axis_size("seq")
    seq_place = lax.axis_index("seq")
    head_width = w_query.shape[1]
    heads_here = head_width // HD
    half_win = WIN // 2
    reach_count = half_win // shard_rows
    my_start = seq_place * shard_rows
    total_tokens = shard_rows * seq_count
    residual = tokens.astype(jnp.float32)
    normed = rms_scale(residual, gain_attn).astype(jnp.bfloat16)
    q_local = jnp.dot(normed, w_query, preferred_element_type=jnp.float32).astype(jnp.bfloat16)
    k_local = jnp.dot(normed, w_key, preferred_element_type=jnp.float32).astype(jnp.bfloat16)
    v_local = jnp.dot(normed, w_value, preferred_element_type=jnp.float32).astype(jnp.bfloat16)
    key_value = jnp.stack([k_local, v_local])
    earlier = [shifted_2(key_value, "seq", distance) for distance in range(reach_count, 0, -1)]
    later = [shifted_2(key_value, "seq", -distance) for distance in range(1, reach_count + 1)]
    window = jnp.concatenate(earlier + [key_value] + later, axis=1)
    span_rows = window.shape[1]
    q_pos = my_start + jnp.arange(shard_rows, dtype=jnp.int32)
    k_pos = my_start - reach_count * shard_rows + jnp.arange(span_rows, dtype=jnp.int32)
    in_window = (
        (jnp.abs(q_pos[:, None] - k_pos[None, :]) <= half_win)
        & (k_pos >= 0)[None, :]
        & (k_pos < total_tokens)[None, :]
    )
    q_heads = q_local.reshape(shard_rows, heads_here, HD)
    k_heads = window[0].reshape(span_rows, heads_here, HD)
    v_heads = window[1].reshape(span_rows, heads_here, HD)
    logits = jnp.einsum(
        "qhd,khd->hqk", q_heads, k_heads, preferred_element_type=jnp.float32
    ) * HD ** (-0.5)
    logits = jnp.where(in_window[None], logits, -jnp.inf)
    row_max = jnp.max(logits, axis=-1, keepdims=True)
    exp_terms = jnp.exp(logits - row_max)
    weights = (exp_terms / jnp.sum(exp_terms, axis=-1, keepdims=True)).astype(jnp.bfloat16)
    mixed = jnp.einsum("hqk,khd->qhd", weights, v_heads, preferred_element_type=jnp.float32)
    mixed = mixed.reshape(shard_rows, head_width).astype(jnp.bfloat16)
    partial_value = jnp.dot(mixed, w_out, preferred_element_type=jnp.float32)
    attn_sum = lax.psum(partial_value, "pb")
    embedded = rms_scale(residual + attn_sum, gain_embed).astype(jnp.bfloat16)
    group_end = jnp.cumsum(group_lengths)
    group_start = group_end - group_lengths
    group_id = jnp.sum((group_end[None, :] <= q_pos[:, None]).astype(jnp.int32), axis=1)
    last_local = jnp.clip(group_end - 1 - my_start, 0, shard_rows - 1)
    present = (group_start < my_start + shard_rows) & (group_end > my_start)
    q_piece = lax.all_gather(queries, "seq", axis=0, tiled=True)
    count = q_piece.shape[0]
    q_rows = q_piece.reshape(count * q_piece.shape[1], q_piece.shape[2])
    similar = jnp.einsum("td,rd->tr", q_rows, embedded, preferred_element_type=jnp.float32)
    running = segmented_max(similar, group_id)
    picked = jnp.take(running, last_local, axis=1)
    picked = jnp.where(present[None, :], picked, -jnp.inf)
    part_max = picked.reshape(count, q_piece.shape[1], picked.shape[-1])
    own_count = queries.shape[0]
    all_maxima = lax.pmax(part_max, "seq")
    token_max = lax.dynamic_slice_in_dim(all_maxima, seq_place * own_count, own_count, 0)
    live_mask = (jnp.arange(LQ, dtype=jnp.int32)[None, :] < query_lengths[:, None]).astype(
        jnp.float32
    )
    scores = (
        jnp.sum(token_max * live_mask[:, :, None], axis=1)
        / query_lengths.astype(jnp.float32)[:, None]
    )
    student_scores = scores / SOFTMAX_TEMP
    student_scores = student_scores - jnp.max(student_scores, axis=-1, keepdims=True)
    student_log_prob = student_scores - jnp.log(
        jnp.sum(jnp.exp(student_scores), axis=-1, keepdims=True)
    )
    target_scores = teacher / SOFTMAX_TEMP
    target_scores = target_scores - jnp.max(target_scores, axis=-1, keepdims=True)
    log_t = target_scores - jnp.log(jnp.sum(jnp.exp(target_scores), axis=-1, keepdims=True))
    teacher_prob = jnp.exp(log_t)
    kl_terms = jnp.sum(teacher_prob * (log_t - student_log_prob), axis=-1)
    query_count_all = own_count * seq_count * lax.axis_size("pb")
    distill_loss = lax.psum(jnp.sum(kl_terms), ("seq", "pb")) / query_count_all
    score_gradient = (jnp.exp(student_log_prob) - teacher_prob) / (SOFTMAX_TEMP * query_count_all)
    return (embedded, scores, score_gradient, distill_loss)


def solution(mesh):
    placed = (
        P("seq", None),
        P(None, "pb"),
        P(None, "pb"),
        P(None, "pb"),
        P("pb", None),
        P(),
        P(),
        P(("seq", "pb"), None, None),
        P(("seq", "pb")),
        P(),
        P(("seq", "pb"), None),
    )
    return jax.shard_map(
        per_device,
        mesh=mesh,
        in_specs=placed,
        out_specs=(P("seq", None), P(("seq", "pb"), None), P(("seq", "pb"), None), P()),
        check_vma=False,
    )
```

profile of v0, /device:TPU:1, one launch (start us, length us, event | category | flops | bytes accessed | tf_op | source)
XLA Modules:
  0.0 512.5 jit_solution(6274992664846566963)
XLA Ops:
  8.1 1.6 fusion.10
  9.8 2.8 fusion.15
  12.6 0.7 fusion.14
  13.4 0.7 copy-done.5
  14.1 0.8 pad_maximum_fusion
  14.9 6.5 %collective-permute-start = (bf16[2,256,512]{2,1,0:T(8,128)(2,1)}, bf16[2,256,512]{2,1,0:T(8,128)(2,1)}, u32[]{:S(2)}, u32[]{:S(2)}) collective-permute-start(bf16[2,256,512]{2,1,0:T(8,128)(2,1)} %pad_maximum_fusion), channel_id=1, source_target_pairs={{0,16},{4,20},{8,24},{12,28},{16,32},{20,36},{24,40},{28,44},{32,4... | collective-permute-start | bytes 1572872 | tf_op jit(solution)/shard_map/ppermute | solution.py:16
  21.5 7.0 %collective-permute-start.1 = (bf16[2,256,512]{2,1,0:T(8,128)(2,1)}, bf16[2,256,512]{2,1,0:T(8,128)(2,1)}, u32[]{:S(2)}, u32[]{:S(2)}) collective-permute-start(bf16[2,256,512]{2,1,0:T(8,128)(2,1)} %pad_maximum_fusion), channel_id=1, source_target_pairs={{0,12},{4,16},{8,20},{12,24},{16,28},{20,32},{24,36},{28,40},{32,4... | collective-permute-start | bytes 1572872 | tf_op jit(solution)/shard_map/ppermute | solution.py:16
  28.4 2.6 collective-permute-start.2
  31.1 1.9 collective-permute-start.3
  33.0 3.2 collective-permute-start.4
  36.3 1.7 fusion.9
  37.9 3.0 fusion.16
  41.0 1.4 collective-permute-start.5
  42.4 1.1 constant_dynamic-update-slice_fusion.8
  43.5 14.3 %collective-permute-done.1 = bf16[2,256,512]{2,1,0:T(8,128)(2,1)} collective-permute-done((bf16[2,256,512]{2,1,0:T(8,128)(2,1)}, bf16[2,256,512]{2,1,0:T(8,128)(2,1)}, u32[]{:S(2)}, u32[]{:S(2)}) %collective-permute-start.1) | collective-permute-done | bytes 524320 | tf_op jit(solution)/shard_map/ppermute | solution.py:16
  57.7 1.3 collective-permute-start.6
  59.0 1.1 constant_dynamic-update-slice_fusion.7
  60.1 10.9 %collective-permute-done.2 = bf16[2,256,512]{2,1,0:T(8,128)(2,1)} collective-permute-done((bf16[2,256,512]{2,1,0:T(8,128)(2,1)}, bf16[2,256,512]{2,1,0:T(8,128)(2,1)}, u32[]{:S(2)}, u32[]{:S(2)}) %collective-permute-start.2) | collective-permute-done | bytes 524320 | tf_op jit(solution)/shard_map/ppermute | solution.py:16
  71.0 1.3 collective-permute-start.7
  72.2 1.1 constant_dynamic-update-slice_fusion.6
  73.3 4.4 collective-permute-done.3
  77.7 1.1 constant_dynamic-update-slice_fusion.5
  78.9 1.1 constant_dynamic-update-slice_fusion.3
  80.0 17.2 %collective-permute-done.6 = bf16[2,256,512]{2,1,0:T(8,128)(2,1)S(1)} collective-permute-done((bf16[2,256,512]{2,1,0:T(8,128)(2,1)}, bf16[2,256,512]{2,1,0:T(8,128)(2,1)S(1)}, u32[]{:S(2)}, u32[]{:S(2)}) %collective-permute-start.6) | collective-permute-done | bytes 524320 | tf_op jit(solution)/shard_map/ppermute | solution.py:16
  97.2 8.1 %collective-permute-done.7 = bf16[2,256,512]{2,1,0:T(8,128)(2,1)S(1)} collective-permute-done((bf16[2,256,512]{2,1,0:T(8,128)(2,1)}, bf16[2,256,512]{2,1,0:T(8,128)(2,1)S(1)}, u32[]{:S(2)}, u32[]{:S(2)}) %collective-permute-start.7) | collective-permute-done | bytes 524320 | tf_op jit(solution)/shard_map/ppermute | solution.py:16
  105.4 2.4 fusion.39
  107.8 4.3 copy.34
  112.1 5.3 %reshape_squeeze.7 = bf16[2304,4,128]{2,1,0:T(4,128)(2,1)} reshape(bf16[1,2304,512]{2,1,0:T(8,128)(2,1)} %get-tuple-element.8) | data formatting | bytes 4718592 | tf_op jit(solution)/shard_map/reshape;squeeze | solution.py:76
  117.4 8.8 %fusion.40 = (f32[4,256]{1,0:T(4,128)S(1)}, f32[4,256,2304]{2,1,0:T(8,128)}) fusion(pred[256,2304]{1,0:T(8,128)(4,1)} %fusion.9, bf16[2304,4,128]{2,1,0:T(4,128)(2,1)} %reshape_squeeze.7, bf16[32,4,8,128]{3,2,1,0:T(8,128)(2,1)S(1)} %copy-done.13), kind=kOutput, calls=%fused_computation.89 | convolution fusion | flops 613419264 | bytes 12652544 | tf_op jit(solution)/shard_map/sub | solution.py:83
  126.2 6.2 %fusion.13 = bf16[4,128,256]{2,1,0:T(8,128)(2,1)S(1)} fusion(bf16[2304,4,128]{0,2,1:T(8,128)(2,1)} %bitcast.54, f32[4,256,2304]{2,1,0:T(8,128)} %get-tuple-element.23, f32[4,256]{1,0:T(4,128)S(1)} %get-tuple-element.22), kind=kOutput, calls=%fused_computation.32 | convolution fusion | flops 608829440 | bytes 12062720 | tf_op jit(solution)/shard_map/hqk,khd->qhd/dot_general | solution.py:85
  132.4 2.0 fusion.45
  134.5 0.5 all-gather.2.cloned.1.call-update
  136.0 66.0 %all-reduce.18.cloned.1.call-done = f32[256,2048]{1,0:T(8,128)} async-done(((f32[256,2048]{1,0:T(8,128)}), f32[256,2048]{1,0:T(8,128)}) %all-reduce.18.cloned.1.call-update) | async-done | bytes 2097168 | tf_op jit(solution)/shard_map/psum | solution.py:88
  202.0 2.1 multiply_reduce_fusion
  204.3 0.4 multiply_convert_fusion
  204.7 20.3 %all-gather.2.cloned.1.call-done = bf16[64,32,2048]{2,1,0:T(8,128)(2,1)} async-done(((bf16[1,32,2048]{2,1,0:T(8,128)(2,1)}), bf16[64,32,2048]{2,1,0:T(8,128)(2,1)}) %all-gather.2.cloned.1.call-update) | async-done | bytes 8388624 | tf_op jit(solution)/shard_map/all_gather | solution.py:95
  225.0 5.7 %convolution_bitcast_fusion = f32[2048,256]{0,1:T(8,128)S(1)} fusion(bf16[256,2048]{1,0:T(8,128)(2,1)S(1)} %multiply_convert_fusion, bf16[2048,2048]{1,0:T(8,128)(2,1)} %bitcast.65), kind=kOutput, calls=%fused_computation.21 | convolution fusion | flops 2147483648 | bytes 11534336 | tf_op jit(solution)/shard_map/td,rd->tr/dot_general | solution.py:98
  234.2 1.0 gather_fusion
  235.2 1.4 copy.33
  236.6 2.4 select_select_fusion
  239.6 0.6 multiply_reduce_fusion.3
  240.3 1.2 exponential_reduce_fusion
  242.2 178.2 %all-reduce.20.cloned.1.call-done = f32[64,32,128]{2,1,0:T(8,128)} async-done(((f32[64,32,128]{2,1,0:T(8,128)}), f32[64,32,128]{2,1,0:T(8,128)}) %all-reduce.20.cloned.1.call-update) | async-done | bytes 1048592 | tf_op jit(solution)/shard_map/pmax | solution.py:104
  420.3 0.8 multiply_reduce_fusion.1
  421.2 0.6 multiply_reduce_fusion.4
  421.8 1.3 exponential_reduce_fusion.1
  423.7 2.5 multiply_reduce_fusion.2
  426.2 77.1 %psum.15 = f32[]{:T(128)} all-reduce(f32[]{:T(128)} %get-tuple-element.10), channel_id=1, replica_groups=mesh['seq'=64,'pb'=4] {'seq','pb'}, use_global_device_ids=true, to_apply=%region_14.15 | all-reduce | flops 1 | bytes 8 | tf_op jit(solution)/shard_map/psum | solution.py:124
  (66 shorter events, 4.8 us)
Async XLA Ops:
  8.0 124.4 %copy-start = (bf16[512,2048]{1,0:T(8,128)(2,1)S(1)}, bf16[512,2048]{1,0:T(8,128)(2,1)}, u32[]{:S(2)}) copy-start(bf16[512,2048]{1,0:T(8,128)(2,1)} %param.15) | copy-start | bytes 6291460
  8.0 194.0 %all-reduce.18.cloned.1.call-start = ((), (), s32[]{:S(2)}) async-start(), calls=%async_computation | async-start | bytes 4194304 | tf_op jit(solution)/shard_map/psum | solution.py:88
  9.7 2.9 copy-start.2
  9.7 2.9 copy-start.11
  9.7 2.9 copy-start.12
  13.4 0.7 copy-start.5
  14.9 26.0 %collective-permute-start = (bf16[2,256,512]{2,1,0:T(8,128)(2,1)}, bf16[2,256,512]{2,1,0:T(8,128)(2,1)}, u32[]{:S(2)}, u32[]{:S(2)}) collective-permute-start(bf16[2,256,512]{2,1,0:T(8,128)(2,1)} %pad_maximum_fusion), channel_id=1, source_target_pairs={{0,16},{4,20},{8,24},{12,28},{16,32},{20,36},{24,40},{28,44},{32,4... | collective-permute-start | bytes 1572872 | tf_op jit(solution)/shard_map/ppermute | solution.py:16
  21.5 36.2 %collective-permute-start.1 = (bf16[2,256,512]{2,1,0:T(8,128)(2,1)}, bf16[2,256,512]{2,1,0:T(8,128)(2,1)}, u32[]{:S(2)}, u32[]{:S(2)}) collective-permute-start(bf16[2,256,512]{2,1,0:T(8,128)(2,1)} %pad_maximum_fusion), channel_id=1, source_target_pairs={{0,12},{4,16},{8,20},{12,24},{16,28},{20,32},{24,36},{28,40},{32,4... | collective-permute-start | bytes 1572872 | tf_op jit(solution)/shard_map/ppermute | solution.py:16
  28.4 42.5 %collective-permute-start.2 = (bf16[2,256,512]{2,1,0:T(8,128)(2,1)}, bf16[2,256,512]{2,1,0:T(8,128)(2,1)}, u32[]{:S(2)}, u32[]{:S(2)}) collective-permute-start(bf16[2,256,512]{2,1,0:T(8,128)(2,1)} %pad_maximum_fusion), channel_id=1, source_target_pairs={{0,8},{4,12},{8,16},{12,20},{16,24},{20,28},{24,32},{28,36},{32,40... | collective-permute-start | bytes 1572872 | tf_op jit(solution)/shard_map/ppermute | solution.py:16
  31.1 46.6 %collective-permute-start.3 = (bf16[2,256,512]{2,1,0:T(8,128)(2,1)}, bf16[2,256,512]{2,1,0:T(8,128)(2,1)}, u32[]{:S(2)}, u32[]{:S(2)}) collective-permute-start(bf16[2,256,512]{2,1,0:T(8,128)(2,1)} %pad_maximum_fusion), channel_id=1, source_target_pairs={{0,4},{4,8},{8,12},{12,16},{16,20},{20,24},{24,28},{28,32},{32,36}... | collective-permute-start | bytes 1572872 | tf_op jit(solution)/shard_map/ppermute | solution.py:16
  33.0 45.9 %collective-permute-start.4 = (bf16[2,256,512]{2,1,0:T(8,128)(2,1)}, bf16[2,256,512]{2,1,0:T(8,128)(2,1)}, u32[]{:S(2)}, u32[]{:S(2)}) collective-permute-start(bf16[2,256,512]{2,1,0:T(8,128)(2,1)} %pad_maximum_fusion), channel_id=1, source_target_pairs={{4,0},{8,4},{12,8},{16,12},{20,16},{24,20},{28,24},{32,28},{36,32}... | collective-permute-start | bytes 1572872 | tf_op jit(solution)/shard_map/ppermute | solution.py:16
  41.0 37.8 %copy-start.6 = (bf16[1,256,512]{2,1,0:T(8,128)(2,1)S(1)}, bf16[1,256,512]{2,1,0:T(8,128)(2,1)}, u32[]{:S(2)}) copy-start(bf16[1,256,512]{2,1,0:T(8,128)(2,1)} %copy-done.5) | copy-start | bytes 786436
  41.0 39.0 %collective-permute-start.5 = (bf16[2,256,512]{2,1,0:T(8,128)(2,1)}, bf16[2,256,512]{2,1,0:T(8,128)(2,1)S(1)}, u32[]{:S(2)}, u32[]{:S(2)}) collective-permute-start(bf16[2,256,512]{2,1,0:T(8,128)(2,1)} %pad_maximum_fusion), channel_id=1, source_target_pairs={{8,0},{12,4},{16,8},{20,12},{24,16},{28,20},{32,24},{36,28},{40,32... | collective-permute-start | bytes 1572872 | tf_op jit(solution)/shard_map/ppermute | solution.py:16
  57.7 39.4 %collective-permute-start.6 = (bf16[2,256,512]{2,1,0:T(8,128)(2,1)}, bf16[2,256,512]{2,1,0:T(8,128)(2,1)S(1)}, u32[]{:S(2)}, u32[]{:S(2)}) collective-permute-start(bf16[2,256,512]{2,1,0:T(8,128)(2,1)} %pad_maximum_fusion), channel_id=1, source_target_pairs={{12,0},{16,4},{20,8},{24,12},{28,16},{32,20},{36,24},{40,28},{44,3... | collective-permute-start | bytes 1572872 | tf_op jit(solution)/shard_map/ppermute | solution.py:16
  71.0 34.4 %collective-permute-start.7 = (bf16[2,256,512]{2,1,0:T(8,128)(2,1)}, bf16[2,256,512]{2,1,0:T(8,128)(2,1)S(1)}, u32[]{:S(2)}, u32[]{:S(2)}) collective-permute-start(bf16[2,256,512]{2,1,0:T(8,128)(2,1)} %pad_maximum_fusion), channel_id=1, source_target_pairs={{16,0},{20,4},{24,8},{28,12},{32,16},{36,20},{40,24},{44,28},{48,3... | collective-permute-start | bytes 1572872 | tf_op jit(solution)/shard_map/ppermute | solution.py:16
  112.1 5.3 %copy-start.13 = (bf16[32,4,8,128]{3,2,1,0:T(8,128)(2,1)S(1)}, bf16[32,4,8,128]{3,2,1,0:T(8,128)(2,1)}, u32[]{:S(2)}) copy-start(bf16[32,4,8,128]{3,2,1,0:T(8,128)(2,1)} %fusion.16) | copy-start | bytes 786436
  134.4 0.8 copy-start.8
  134.4 69.7 %copy-start.7 = (f32[2048]{0:T(1024)S(1)}, f32[2048]{0:T(1024)}, u32[]{:S(2)}) copy-start(f32[2048]{0:T(1024)} %param.17) | copy-start | bytes 24580
  134.5 90.5 %all-gather.2.cloned.1.call-start = ((), (), s32[]{:S(2)}) async-start(), calls=%async_computation.1 | async-start | bytes 8519680 | tf_op jit(solution)/shard_map/all_gather | solution.py:95
  135.0 285.3 %all-reduce.20.cloned.1.call-start = ((), (), s32[]{:S(2)}) async-start(), calls=%async_computation.2 | async-start | bytes 2097152 | tf_op jit(solution)/shard_map/pmax | solution.py:104
  202.0 2.3 copy-start.3
  204.6 26.1 %copy-start.4 = (bf16[256,2048]{1,0:T(8,128)(2,1)}, bf16[256,2048]{1,0:T(8,128)(2,1)S(1)}, u32[]{:S(2)}) copy-start(bf16[256,2048]{1,0:T(8,128)(2,1)S(1)} %multiply_convert_fusion) | copy-start | bytes 3145732
  235.2 268.7 %copy-start.1 = (bf16[512,2048]{1,0:T(8,128)(2,1)S(1)}, bf16[512,2048]{1,0:T(8,128)(2,1)}, u32[]{:S(2)}) copy-start(bf16[512,2048]{1,0:T(8,128)(2,1)} %param.15) | copy-start | bytes 6291460
  236.6 3.0 copy-start.10
  421.8 82.2 %copy-start.9 = (f32[128]{0:T(128)}, f32[128]{0:T(128)S(1)}, u32[]{:S(2)}) copy-start(f32[128]{0:T(128)S(1)} %get-tuple-element.7) | copy-start | bytes 1540
Sparse Core Ops, SparseCore 0:
  134.6 67.3 all-reduce.17
Sparse Core Ops, SparseCore 1:
  137.7 87.2 all-gather.1
  239.1 181.2 all-reduce.19
where the time goes:
time: 514 us; the launch traced here: 513 us
  waiting for transfers between devices  320 us (62%)
  blocking collectives  77.1 us (15%)
  matrix products  29.3 us (6%)
  starting transfers between devices  25.5 us (5%)
  local copies, waits for them, and re-layouts  21.7 us (4%)
  between operations  19.7 us (4%)
  other arithmetic  19.2 us (4%)
    pmax x1, waiting for transfers between devices, per_device(): all_maxima = lax.pmax(part_max, 'seq')  178 us
    psum x1, blocking collectives, per_device(): distill_loss = lax.psum(jnp.sum(kl_terms), ('seq', 'pb')) / query_count_all  77.1 us
    psum x1, waiting for transfers between devices, per_device(): attn_sum = lax.psum(partial_value, 'pb')  66 us
    ppermute x8, waiting for transfers between devices, shifted_2(): return lax.ppermute(x, axis, pairs)  54.8 us
    ppermute x8, starting transfers between devices, shifted_2(): return lax.ppermute(x, axis, pairs)  25.2 us
    all_gather x1, waiting for transfers between devices, per_device(): q_piece = lax.all_gather(queries, 'seq', axis=0, tiled=True)  20.3 us
  transfers between devices with their start and end apart: 11, of which 8 were waited for; matrix products, arithmetic and copies ran while one was open for 3% of the time, Pallas kernels for 0%

commit v1 on v0

--- a/solution.py
+++ b/solution.py
@@ -92,7 +92,9 @@
     group_id = jnp.sum((group_end[None, :] <= q_pos[:, None]).astype(jnp.int32), axis=1)
     last_local = jnp.clip(group_end - 1 - my_start, 0, shard_rows - 1)
     present = (group_start < my_start + shard_rows) & (group_end > my_start)
-    q_piece = lax.all_gather(queries, "seq", axis=0, tiled=True)
+    q_piece = jnp.concatenate(
+        lax.all_to_all(jnp.stack([queries] * lax.axis_size("seq")), "seq", 0, 0), axis=0
+    )
     count = q_piece.shape[0]
     q_rows = q_piece.reshape(count * q_piece.shape[1], q_piece.shape[2])
     similar = jnp.einsum("td,rd->tr", q_rows, embedded, preferred_element_type=jnp.float32)

time: 514 us -> 682 us (1.33)
  waiting for transfers between devices: 320 us -> 474 us
  starting transfers between devices: 25.5 us -> 35.8 us
    ppermute x8, waiting for transfers between devices: 54.8 us -> 227 us  [shifted_2(): return lax.ppermute(x, axis, pairs)]
    all_gather x1 -> x0, waiting for transfers between devices: 20.3 us -> none  [per_device(): q_piece = lax.all_gather(queries, 'seq', axis=0, tiled=True)]
    all_to_all x0 -> x1, starting transfers between devices: none -> 13.5 us  [per_device(): lax.all_to_all(jnp.stack([queries] * lax.axis_size('seq')), 'seq', 0, 0)]
  transfers between devices with their start and end apart: 11 -> 11, of which waited for: 8 -> 8; matrix products, arithmetic and copies ran while one was open for 3% -> 7% of each run, Pallas kernels for 0% -> 0%
where the time goes in v1:
time: 682 us; the launch traced here: 681 us
  waiting for transfers between devices  474 us (70%)
  blocking collectives  77.2 us (11%)
  starting transfers between devices  35.8 us (5%)
  matrix products  29.3 us (4%)
  local copies, waits for them, and re-layouts  27.3 us (4%)
  other arithmetic  18.8 us (3%)
  between operations  18.3 us (3%)
    ppermute x8, waiting for transfers between devices, shifted_2(): return lax.ppermute(x, axis, pairs)  227 us
    pmax x1, waiting for transfers between devices, per_device(): all_maxima = lax.pmax(part_max, 'seq')  182 us
    psum x1, blocking collectives, per_device(): distill_loss = lax.psum(jnp.sum(kl_terms), ('seq', 'pb')) / query_count_all  77.2 us
    psum x1, waiting for transfers between devices, per_device(): attn_sum = lax.psum(partial_value, 'pb')  64.8 us
    ppermute x8, starting transfers between devices, shifted_2(): return lax.ppermute(x, axis, pairs)  22 us
  transfers between devices with their start and end apart: 11, of which 8 were waited for; matrix products, arithmetic and copies ran while one was open for 7% of the time, Pallas kernels for 0%

profile of v1, /device:TPU:1, one launch (start us, length us, event | category | flops | bytes accessed | tf_op | source)
XLA Modules:
  0.0 681.0 jit_solution(9934922077729418531)
XLA Ops:
  7.2 5.4 stack.11
  12.6 13.5 %all-to-all-start = ((bf16[64,1,32,2048]{3,2,1,0:T(8,128)(2,1)}), bf16[64,1,32,2048]{3,2,1,0:T(8,128)(2,1)}, u32[]{:S(2)}, u32[]{:S(2)}) async-start(bf16[64,1,32,2048]{3,2,1,0:T(8,128)(2,1)} %stack.11), calls=%async_computation | async-start | bytes 16777216 | tf_op jit(solution)/shard_map/all_to_all | solution.py:96
  26.5 2.5 fusion.14
  29.0 0.8 fusion.15
  29.7 0.7 copy-done.4
  30.5 0.8 pad_maximum_fusion
  31.3 5.0 collective-permute-start
  36.3 5.8 collective-permute-start.1
  42.0 2.2 collective-permute-start.2
  44.2 1.9 collective-permute-start.3
  46.1 3.2 collective-permute-start.4
  49.4 1.7 fusion.9
  51.0 3.1 fusion.16
  54.1 174.2 %collective-permute-done = bf16[2,256,512]{2,1,0:T(8,128)(2,1)} collective-permute-done((bf16[2,256,512]{2,1,0:T(8,128)(2,1)}, bf16[2,256,512]{2,1,0:T(8,128)(2,1)}, u32[]{:S(2)}, u32[]{:S(2)}) %collective-permute-start) | collective-permute-done | bytes 524320 | tf_op jit(solution)/shard_map/ppermute | solution.py:16
  228.3 1.3 collective-permute-start.5
  229.6 1.1 constant_dynamic-update-slice_fusion.8
  230.7 13.6 %collective-permute-done.1 = bf16[2,256,512]{2,1,0:T(8,128)(2,1)} collective-permute-done((bf16[2,256,512]{2,1,0:T(8,128)(2,1)}, bf16[2,256,512]{2,1,0:T(8,128)(2,1)}, u32[]{:S(2)}, u32[]{:S(2)}) %collective-permute-start.1) | collective-permute-done | bytes 524320 | tf_op jit(solution)/shard_map/ppermute | solution.py:16
  244.3 1.3 collective-permute-start.6
  245.6 1.1 constant_dynamic-update-slice_fusion.7
  246.7 9.9 %collective-permute-done.2 = bf16[2,256,512]{2,1,0:T(8,128)(2,1)} collective-permute-done((bf16[2,256,512]{2,1,0:T(8,128)(2,1)}, bf16[2,256,512]{2,1,0:T(8,128)(2,1)}, u32[]{:S(2)}, u32[]{:S(2)}) %collective-permute-start.2) | collective-permute-done | bytes 524320 | tf_op jit(solution)/shard_map/ppermute | solution.py:16
  256.6 1.5 collective-permute-start.7
  258.0 1.1 constant_dynamic-update-slice_fusion.6
  259.1 3.6 collective-permute-done.3
  262.7 1.1 constant_dynamic-update-slice_fusion.5
  263.8 1.1 constant_dynamic-update-slice_fusion.3
  265.0 3.8 collective-permute-done.6
  268.8 22.1 %collective-permute-done.7 = bf16[2,256,512]{2,1,0:T(8,128)(2,1)S(1)} collective-permute-done((bf16[2,256,512]{2,1,0:T(8,128)(2,1)}, bf16[2,256,512]{2,1,0:T(8,128)(2,1)S(1)}, u32[]{:S(2)}, u32[]{:S(2)}) %collective-permute-start.7) | collective-permute-done | bytes 524320 | tf_op jit(solution)/shard_map/ppermute | solution.py:16
  291.0 2.4 fusion.39
  293.4 5.3 reshape_squeeze.7
  298.7 4.4 copy.29
  303.0 8.8 %fusion.40 = (f32[4,256]{1,0:T(4,128)S(1)}, f32[4,256,2304]{2,1,0:T(8,128)}) fusion(pred[256,2304]{1,0:T(8,128)(4,1)} %fusion.9, bf16[2304,4,128]{2,1,0:T(4,128)(2,1)} %reshape_squeeze.7, bf16[32,4,8,128]{3,2,1,0:T(8,128)(2,1)S(1)} %copy-done.12), kind=kOutput, calls=%fused_computation.89 | convolution fusion | flops 613419264 | bytes 12652544 | tf_op jit(solution)/shard_map/sub | solution.py:83
  311.8 6.2 fusion.13
  318.0 2.0 fusion.45
  321.4 64.8 %all-reduce.18.cloned.1.call-done = f32[256,2048]{1,0:T(8,128)} async-done(((f32[256,2048]{1,0:T(8,128)}), f32[256,2048]{1,0:T(8,128)}) %all-reduce.18.cloned.1.call-update) | async-done | bytes 2097168 | tf_op jit(solution)/shard_map/psum | solution.py:88
  386.2 2.1 multiply_reduce_fusion
  388.4 1.3 multiply_convert_fusion
  389.7 6.1 convolution_bitcast_fusion
  399.1 1.0 gather_fusion
  400.1 1.4 copy.28
  401.5 2.4 select_select_fusion
  404.5 0.6 multiply_reduce_fusion.3
  405.2 1.2 exponential_reduce_fusion
  407.1 182.3 %all-reduce.20.cloned.1.call-done = f32[64,32,128]{2,1,0:T(8,128)} async-done(((f32[64,32,128]{2,1,0:T(8,128)}), f32[64,32,128]{2,1,0:T(8,128)}) %all-reduce.20.cloned.1.call-update) | async-done | bytes 1048592 | tf_op jit(solution)/shard_map/pmax | solution.py:106
  589.4 0.8 multiply_reduce_fusion.1
  590.2 0.6 multiply_reduce_fusion.4
  590.8 1.3 exponential_reduce_fusion.1
  592.7 2.5 multiply_reduce_fusion.2
  595.2 77.2 %psum.15 = f32[]{:T(128)} all-reduce(f32[]{:T(128)} %get-tuple-element.10), channel_id=1, replica_groups=mesh['seq'=64,'pb'=4] {'seq','pb'}, use_global_device_ids=true, to_apply=%region_14.15 | all-reduce | flops 1 | bytes 8 | tf_op jit(solution)/shard_map/psum | solution.py:126
  (64 shorter events, 5.3 us)
Async XLA Ops:
  7.2 310.8 %copy-start = (bf16[512,2048]{1,0:T(8,128)(2,1)S(1)}, bf16[512,2048]{1,0:T(8,128)(2,1)}, u32[]{:S(2)}) copy-start(bf16[512,2048]{1,0:T(8,128)(2,1)} %param.15) | copy-start | bytes 6291460
  12.6 13.5 %copy-start.2 = (bf16[256,2048]{1,0:T(8,128)(2,1)S(1)}, bf16[256,2048]{1,0:T(8,128)(2,1)}, u32[]{:S(2)}) copy-start(bf16[256,2048]{1,0:T(8,128)(2,1)} %param.11) | copy-start | bytes 3145732
  12.6 13.8 %copy-start.11 = (f32[2048]{0:T(1024)S(1)}, f32[2048]{0:T(1024)}, u32[]{:S(2)}) copy-start(f32[2048]{0:T(1024)} %param.16) | copy-start | bytes 24580
  12.6 377.1 %all-to-all-start = ((bf16[64,1,32,2048]{3,2,1,0:T(8,128)(2,1)}), bf16[64,1,32,2048]{3,2,1,0:T(8,128)(2,1)}, u32[]{:S(2)}, u32[]{:S(2)}) async-start(bf16[64,1,32,2048]{3,2,1,0:T(8,128)(2,1)} %stack.11), calls=%async_computation | async-start | bytes 16777216 | tf_op jit(solution)/shard_map/all_to_all | solution.py:96
  26.1 360.1 %all-reduce.18.cloned.1.call-start = ((), (), s32[]{:S(2)}) async-start(), calls=%async_computation.1 | async-start | bytes 4194304 | tf_op jit(solution)/shard_map/psum | solution.py:88
  26.4 2.5 copy-start.10
  29.7 0.7 copy-start.4
  31.3 197.1 %collective-permute-start = (bf16[2,256,512]{2,1,0:T(8,128)(2,1)}, bf16[2,256,512]{2,1,0:T(8,128)(2,1)}, u32[]{:S(2)}, u32[]{:S(2)}) collective-permute-start(bf16[2,256,512]{2,1,0:T(8,128)(2,1)} %pad_maximum_fusion), channel_id=1, source_target_pairs={{0,16},{4,20},{8,24},{12,28},{16,32},{20,36},{24,40},{28,44},{32,4... | collective-permute-start | bytes 1572872 | tf_op jit(solution)/shard_map/ppermute | solution.py:16
  36.3 208.0 %collective-permute-start.1 = (bf16[2,256,512]{2,1,0:T(8,128)(2,1)}, bf16[2,256,512]{2,1,0:T(8,128)(2,1)}, u32[]{:S(2)}, u32[]{:S(2)}) collective-permute-start(bf16[2,256,512]{2,1,0:T(8,128)(2,1)} %pad_maximum_fusion), channel_id=1, source_target_pairs={{0,12},{4,16},{8,20},{12,24},{16,28},{20,32},{24,36},{28,40},{32,4... | collective-permute-start | bytes 1572872 | tf_op jit(solution)/shard_map/ppermute | solution.py:16
  42.0 214.5 %collective-permute-start.2 = (bf16[2,256,512]{2,1,0:T(8,128)(2,1)}, bf16[2,256,512]{2,1,0:T(8,128)(2,1)}, u32[]{:S(2)}, u32[]{:S(2)}) collective-permute-start(bf16[2,256,512]{2,1,0:T(8,128)(2,1)} %pad_maximum_fusion), channel_id=1, source_target_pairs={{0,8},{4,12},{8,16},{12,20},{16,24},{20,28},{24,32},{28,36},{32,40... | collective-permute-start | bytes 1572872 | tf_op jit(solution)/shard_map/ppermute | solution.py:16
  44.2 218.5 %collective-permute-start.3 = (bf16[2,256,512]{2,1,0:T(8,128)(2,1)}, bf16[2,256,512]{2,1,0:T(8,128)(2,1)}, u32[]{:S(2)}, u32[]{:S(2)}) collective-permute-start(bf16[2,256,512]{2,1,0:T(8,128)(2,1)} %pad_maximum_fusion), channel_id=1, source_target_pairs={{0,4},{4,8},{8,12},{12,16},{16,20},{20,24},{24,28},{28,32},{32,36}... | collective-permute-start | bytes 1572872 | tf_op jit(solution)/shard_map/ppermute | solution.py:16
  46.1 217.7 %collective-permute-start.4 = (bf16[2,256,512]{2,1,0:T(8,128)(2,1)}, bf16[2,256,512]{2,1,0:T(8,128)(2,1)}, u32[]{:S(2)}, u32[]{:S(2)}) collective-permute-start(bf16[2,256,512]{2,1,0:T(8,128)(2,1)} %pad_maximum_fusion), channel_id=1, source_target_pairs={{4,0},{8,4},{12,8},{16,12},{20,16},{24,20},{28,24},{32,28},{36,32}... | collective-permute-start | bytes 1572872 | tf_op jit(solution)/shard_map/ppermute | solution.py:16
  54.1 209.7 %copy-start.5 = (bf16[1,256,512]{2,1,0:T(8,128)(2,1)S(1)}, bf16[1,256,512]{2,1,0:T(8,128)(2,1)}, u32[]{:S(2)}) copy-start(bf16[1,256,512]{2,1,0:T(8,128)(2,1)} %copy-done.4) | copy-start | bytes 786436
  228.3 36.6 %collective-permute-start.5 = (bf16[2,256,512]{2,1,0:T(8,128)(2,1)}, bf16[2,256,512]{2,1,0:T(8,128)(2,1)S(1)}, u32[]{:S(2)}, u32[]{:S(2)}) collective-permute-start(bf16[2,256,512]{2,1,0:T(8,128)(2,1)} %pad_maximum_fusion), channel_id=1, source_target_pairs={{8,0},{12,4},{16,8},{20,12},{24,16},{28,20},{32,24},{36,28},{40,32... | collective-permute-start | bytes 1572872 | tf_op jit(solution)/shard_map/ppermute | solution.py:16
  244.3 24.5 %collective-permute-start.6 = (bf16[2,256,512]{2,1,0:T(8,128)(2,1)}, bf16[2,256,512]{2,1,0:T(8,128)(2,1)S(1)}, u32[]{:S(2)}, u32[]{:S(2)}) collective-permute-start(bf16[2,256,512]{2,1,0:T(8,128)(2,1)} %pad_maximum_fusion), channel_id=1, source_target_pairs={{12,0},{16,4},{20,8},{24,12},{28,16},{32,20},{36,24},{40,28},{44,3... | collective-permute-start | bytes 1572872 | tf_op jit(solution)/shard_map/ppermute | solution.py:16
  256.6 34.4 %collective-permute-start.7 = (bf16[2,256,512]{2,1,0:T(8,128)(2,1)}, bf16[2,256,512]{2,1,0:T(8,128)(2,1)S(1)}, u32[]{:S(2)}, u32[]{:S(2)}) collective-permute-start(bf16[2,256,512]{2,1,0:T(8,128)(2,1)} %pad_maximum_fusion), channel_id=1, source_target_pairs={{16,0},{20,4},{24,8},{28,12},{32,16},{36,20},{40,24},{44,28},{48,3... | collective-permute-start | bytes 1572872 | tf_op jit(solution)/shard_map/ppermute | solution.py:16
  298.7 4.4 copy-start.12
  320.0 0.7 copy-start.7
  320.0 68.2 %copy-start.6 = (f32[2048]{0:T(1024)S(1)}, f32[2048]{0:T(1024)}, u32[]{:S(2)}) copy-start(f32[2048]{0:T(1024)} %param.17) | copy-start | bytes 24580
  320.1 269.3 %all-reduce.20.cloned.1.call-start = ((), (), s32[]{:S(2)}) async-start(), calls=%async_computation.2 | async-start | bytes 2097152 | tf_op jit(solution)/shard_map/pmax | solution.py:106
  386.2 2.2 copy-start.3
  400.1 272.9 %copy-start.1 = (bf16[512,2048]{1,0:T(8,128)(2,1)S(1)}, bf16[512,2048]{1,0:T(8,128)(2,1)}, u32[]{:S(2)}) copy-start(bf16[512,2048]{1,0:T(8,128)(2,1)} %param.15) | copy-start | bytes 6291460
  401.5 3.0 copy-start.9
  590.8 82.3 %copy-start.8 = (f32[128]{0:T(128)}, f32[128]{0:T(128)S(1)}, u32[]{:S(2)}) copy-start(f32[128]{0:T(128)S(1)} %get-tuple-element.7) | copy-start | bytes 1540
Sparse Core Ops, SparseCore 0:
  320.2 65.9 all-reduce.17
  404.0 185.3 all-reduce.19
